TPU v7x, 512 devices: a whole 4x8x8 slice. The times are simulated.
512 devices in a mesh: atom: 64 (over y, x, z_hi), ka: 8 (over z_lo, core).
Axes of the slice: x: 4, y: 8, z: 8 (z_hi: 2, z_lo: 4; z = z_hi * 4 + z_lo), core: 2. Of those that a mesh axis runs over, the one named last changes fastest.
Arguments:
- features: bfloat16 [131072, 256], P('atom'), may hold values from -6 to 6
- positions: float32 [3, 131072], P(None, 'atom'), may hold values from 0 to 1
- k_indices: int32 [3, 4096], P(None, 'ka'), may hold values from -8 to 8
- species: int32 [131072], P('atom'), may hold values from 0 to 7
- brick_counts: int32 [64], P('atom'), may hold values from 1024 to 2048, as said below
- smearing: float32 [256], replicated, may hold values from 0.01 to 0.03
- teacher_charge: float32 [256], replicated, may hold values from -0.375 to 0.375
- norm_gain: float32 [256], replicated, may hold values from 0.5 to 1.5
- w_mix: bfloat16 [256, 256], replicated, may hold values from -0.375 to 0.375
- w_read: float32 [256], replicated, may hold values from -0.375 to 0.375
- w_student: bfloat16 [256, 128], replicated, may hold values from -0.375 to 0.375
- species_embed: float32 [8, 128], replicated, may hold values from -3 to 3
- w_charge: float32 [128], replicated, may hold values from -0.5 to 0.5
- species_bias: float32 [8], replicated, may hold values from -3 to 3
- student_smear: float32 [1], replicated, may hold values from 0.05 to 0.15
Outputs:
- teacher_features: bfloat16 [131072, 256], P(('atom', 'ka'))
- teacher_forces: float32 [3, 131072], P(None, ('atom', 'ka'))
- student_forces: float32 [3, 131072], P(None, ('atom', 'ka'))
- student_energy: float32 [131072], P(('atom', 'ka'))
- distill_loss: float32 [], replicated
Inputs may be any that keep to these rules, and one draw needn't show every extreme that they name: The first brick_counts[b] atom slots of brick b hold real atoms and the rest are padding; some brick is full in every draw.
All inputs are finite; a program needn't handle non-finite values.
Results may differ from a plain program's by a relative error of at most 0.0075.
Values sent between devices are 32-bit elements; how exact they have to be, the bound alone decides.
No kernel may reach another device: no remote copies, remote signals or barrier semaphores. Data moves between devices by JAX's collectives and lax.ppermute only.
A program may use at most 64 MiB of HBM per device.

v0:
```python
import math
import jax
import jax.numpy as jnp
from jax import lax
from jax.sharding import PartitionSpec as P

TWO_PI = 2.0 * math.pi
SCREEN = 20.0
HIGHEST_PRECISION = lax.Precision.HIGHEST


def phase_table(positions, k_indices):
    k_float = k_indices.astype(jnp.float32)
    products = (
        positions[0][:, None] * k_float[0][None, :]
        + positions[1][:, None] * k_float[1][None, :]
        + positions[2][:, None] * k_float[2][None, :]
    )
    angles = TWO_PI * products
    return jnp.concatenate([jnp.cos(angles), jnp.sin(angles)], axis=1).astype(jnp.bfloat16)


def k_geometry(k_indices):
    k_vectors = TWO_PI * k_indices.astype(jnp.float32)
    k_square = (
        k_vectors[0] * k_vectors[0] + k_vectors[1] * k_vectors[1] + k_vectors[2] * k_vectors[2]
    )
    return (k_vectors, k_square)


def teacher_kernel(k_square, smearing, inv_root):
    spread = (smearing * smearing)[None, :]
    return jnp.exp(-0.5 * k_square[:, None] * spread) / (k_square[:, None] + SCREEN) * inv_root


def student_table(k_vectors, k_square, sums, student_smear, inv_root, k_width):
    spread = student_smear[0] * student_smear[0]
    kernel = jnp.exp(-0.5 * k_square * spread) / (k_square + SCREEN) * inv_root
    cos_part = kernel * sums[:k_width]
    sin_part = kernel * sums[k_width:]
    upper_rows = jnp.stack(
        [
            cos_part,
            -(k_vectors[0] * sin_part),
            -(k_vectors[1] * sin_part),
            -(k_vectors[2] * sin_part),
        ],
        axis=1,
    )
    lower_rows = jnp.stack(
        [sin_part, k_vectors[0] * cos_part, k_vectors[1] * cos_part, k_vectors[2] * cos_part],
        axis=1,
    )
    return jnp.concatenate([upper_rows, lower_rows], axis=0).astype(jnp.bfloat16)


def student_charge(features, species, live_mask, w_student, species_embed, w_charge, species_bias):
    onehot = (
        species[:, None] == jnp.arange(species_embed.shape[0], dtype=jnp.int32)[None, :]
    ).astype(jnp.float32)
    inner_sum = jnp.dot(features, w_student, preferred_element_type=jnp.float32) + jnp.dot(
        onehot, species_embed, precision=HIGHEST_PRECISION
    )
    hidden = jax.nn.silu(inner_sum)
    return (
        jnp.dot(hidden, w_charge, precision=HIGHEST_PRECISION)
        + jnp.dot(onehot, species_bias, precision=HIGHEST_PRECISION)
    ) * live_mask


def finish(
    potential, teacher_force, student_part, features, charge, live_mask, norm_gain, w_mix, w_read
):
    mean_square = jnp.mean(potential * potential, axis=1, keepdims=True)
    normed = (potential * lax.rsqrt(mean_square + 1e-06) * norm_gain[None, :]).astype(jnp.bfloat16)
    update = jax.nn.silu(jnp.dot(normed, w_mix, preferred_element_type=jnp.float32))
    combined = features.astype(jnp.float32) + update
    teacher_energy = jnp.dot(combined, w_read, precision=HIGHEST_PRECISION)
    student_energy = 0.5 * charge * student_part[:, 0]
    forces = charge[:, None] * student_part[:, 1:4]
    misfit = (student_energy - teacher_energy) ** 2 + jnp.sum(
        (forces - teacher_force) ** 2, axis=1
    ) / 3.0
    return (
        combined.astype(jnp.bfloat16),
        teacher_force,
        forces,
        student_energy,
        live_mask * misfit,
    )


def local(
    features,
    positions,
    k_indices,
    species,
    brick_counts,
    smearing,
    teacher_charge,
    norm_gain,
    w_mix,
    w_read,
    w_student,
    species_embed,
    w_charge,
    species_bias,
    student_smear,
):
    atom_rows = features.shape[0]
    k_width = k_indices.shape[1]
    inv_root = 1.0 / math.sqrt(atom_rows * lax.axis_size("atom"))
    live_mask = (jnp.arange(atom_rows, dtype=jnp.int32) < brick_counts[0]).astype(jnp.float32)
    masked = features * live_mask.astype(jnp.bfloat16)[:, None]
    charge = student_charge(
        features, species, live_mask, w_student, species_embed, w_charge, species_bias
    )
    charge_low = charge.astype(jnp.bfloat16)
    phases = phase_table(positions, k_indices)
    factor = lax.dot_general(
        phases, masked, (((0,), (0,)), ((), ())), preferred_element_type=jnp.float32
    )
    charge_sum = jnp.dot(charge_low, phases, preferred_element_type=jnp.float32)
    factor, charge_sum = lax.psum((factor, charge_sum), "atom")
    k_vectors, k_square = k_geometry(k_indices)
    kernel = teacher_kernel(k_square, smearing, inv_root)
    weighted = (jnp.concatenate([kernel, kernel], axis=0) * factor).astype(jnp.bfloat16)
    potential = jnp.dot(phases, weighted, preferred_element_type=jnp.float32)
    charged = (features.astype(jnp.float32) * teacher_charge[None, :]).astype(jnp.bfloat16)
    contracted = lax.dot_general(
        charged, weighted, (((1,), (1,)), ((), ())), preferred_element_type=jnp.float32
    )
    cosines = phases[:, :k_width].astype(jnp.float32)
    sines = phases[:, k_width:].astype(jnp.float32)
    force_terms = sines * contracted[:, :k_width] - cosines * contracted[:, k_width:]
    teacher_force = jnp.dot(force_terms, k_vectors.T, precision=HIGHEST_PRECISION)
    table = student_table(k_vectors, k_square, charge_sum, student_smear, inv_root, k_width)
    student_part = jnp.dot(phases, table, preferred_element_type=jnp.float32)
    share_rows = atom_rows // lax.axis_size("ka")
    row_start = lax.axis_index("ka") * share_rows

    def own_rows(values):
        return lax.dynamic_slice_in_dim(values, row_start, share_rows, 0)

    potential, teacher_force, student_part = lax.psum(
        (potential, teacher_force, student_part), "ka"
    )
    whole_rows = finish(
        potential,
        teacher_force,
        student_part,
        features,
        charge,
        live_mask,
        norm_gain,
        w_mix,
        w_read,
    )
    outputs = (
        own_rows(whole_rows[0]),
        own_rows(whole_rows[1]),
        own_rows(whole_rows[2]),
        own_rows(whole_rows[3]),
        own_rows(whole_rows[4]),
    )
    teacher_features, teacher_out, forces, student_energy, misfit = outputs
    loss_sum, live_sum = lax.psum((jnp.sum(misfit), jnp.sum(own_rows(live_mask))), ("atom", "ka"))
    return (teacher_features, teacher_out.T, forces.T, student_energy, loss_sum / live_sum)


def solution(mesh):
    in_specs = (
        P("atom", None),
        P(None, "atom"),
        P(None, "ka"),
        P("atom"),
        P("atom"),
        P(),
        P(),
        P(),
        P(),
        P(),
        P(),
        P(),
        P(),
        P(),
        P(),
    )
    out_specs = (
        P(("atom", "ka"), None),
        P(None, ("atom", "ka")),
        P(None, ("atom", "ka")),
        P(("atom", "ka")),
        P(),
    )
    return jax.shard_map(local, mesh=mesh, in_specs=in_specs, out_specs=out_specs, check_vma=False)
```

profile of v0, /device:TPU:1, one launch (start us, length us, event | category | flops | bytes accessed | tf_op | source)
XLA Modules:
  0.0 1086.3 jit_solution(1658053746841825445)
XLA Ops:
  7.2 0.0 copy-start
  7.2 0.0 copy-start.1
  7.2 0.0 all-reduce.5.cloned.1.call-start
  8.0 0.7 convert_element_type.47
  8.7 0.9 fusion.58
  9.6 17.6 %cosine_convert_fusion = (bf16[2048,512]{1,0:T(8,128)(2,1)S(1)}, bf16[2048,512]{1,0:T(8,128)(2,1)S(1)}) fusion(f32[512]{0:T(512)S(1)} %bitcast.54, f32[2048]{0:T(1024)S(1)} %bitcast.39, f32[512]{0:T(512)S(1)} %bitcast.56, f32[2048]{0:T(1024)S(1)} %bitcast.41, f32[512]{0:T(512)S(1)} %bitcast.52, f32[2048]{0:T(1024)S(1)} %bitcast.37), kind=kLoop, calls=%fused_computation.8 | loop fusion | flops 8388608 | bytes 4225024 | tf_op jit(solution)/shard_map/slice | solution.py:133
  27.2 0.0 copy-start.3
  27.2 0.0 copy-start.2
  27.3 1.3 copy-done.3
  28.6 0.0 copy-done.1
  28.6 0.0 copy-start.10
  28.6 0.0 copy-start.6
  28.6 0.0 copy-start.8
  28.6 0.0 copy-start.14
  28.6 0.0 copy-start.9
  28.6 2.6 fusion.20
  31.2 0.0 copy-start.15
  31.2 0.0 all-reduce.5.cloned.1.call-update
  31.3 0.0 all-reduce.7.cloned.1.call-start
  32.0 0.0 copy-done.10
  32.0 0.0 copy-done.6
  32.0 0.0 copy-start.4
  32.0 0.4 fusion.61
  32.4 0.0 copy-done.8
  32.4 0.0 copy-done.14
  32.4 0.7 fusion.16
  33.2 0.0 copy-done.9
  33.2 1.0 convolution_add_fusion
  34.1 0.0 copy-done.15
  34.1 0.0 copy-start.7
  34.2 1.2 fusion.10
  35.4 0.0 copy-done.2
  35.4 0.0 copy-done.4
  35.4 0.6 fusion.55
  36.0 203.7 %psum.52 = f32[1024]{0:T(1024)S(1)} all-reduce(f32[1024]{0:T(1024)S(1)} %bitcast.60), channel_id=1, replica_groups=mesh['atom'=64,'ka'=8] {'atom'}, use_global_device_ids=true, to_apply=%region_4.5 | all-reduce | flops 1024 | bytes 8192 | tf_op jit(solution)/shard_map/psum | solution.py:124
  239.7 0.0 copy-done.7
  239.8 0.2 divide_multiply_fusion
  240.0 599.3 %all-reduce.5.cloned.1.call-done = f32[1024,256]{1,0:T(8,128)} async-done(((f32[1024,256]{1,0:T(8,128)}), f32[1024,256]{1,0:T(8,128)}) %all-reduce.5.cloned.1.call-update) | async-done | bytes 1048592 | tf_op jit(solution)/shard_map/psum | solution.py:124
  839.4 5.1 fusion.53
  844.5 0.0 all-reduce.7.cloned.1.call-update
  844.6 0.7 dynamic-slice_reduce_fusion
  845.3 0.0 copy-start.5
  845.3 0.0 copy-start.11
  845.3 3.5 fusion.26
  848.8 0.0 copy-done.5
  848.8 0.0 copy-done.11
  848.8 1.3 fusion.7
  850.1 0.0 copy-start.13
  850.1 20.6 %fusion.1 = f32[2048,3]{0,1:T(4,128)S(1)} fusion(f32[2048,1024]{1,0:T(8,128)S(1)} %fusion.7, s32[3,512]{1,0:T(4,128)S(1)} %copy-done.7, f32[512]{0:T(512)S(1)} %bitcast.55, f32[2048]{0:T(1024)S(1)} %bitcast.40, f32[512]{0:T(512)S(1)} %bitcast.57, f32[2048]{0:T(1024)S(1)} %bitcast.42, f32[512]{0:T(512)S(1)} %bitcast.53, f32[2048]{0:T(1024)S(1)} %bitcast.38), kind=kOutput, calls=%fused_computation.2 | convolution fusion | flops 51383296 | bytes 8450048 | tf_op jit(solution)/shard_map/dot_general | solution.py:136
  870.8 68.6 %all-reduce.1 = (f32[2048,3]{0,1:T(4,128)S(1)}, f32[2048,4]{0,1:T(4,128)S(1)}) all-reduce(f32[2048,3]{0,1:T(4,128)S(1)} %fusion.1, f32[2048,4]{0,1:T(4,128)S(1)} %fusion.26), channel_id=1, replica_groups=mesh['atom'=64,'ka'=8] {'ka'}, use_global_device_ids=true, to_apply=%region_3.4 | all-reduce | flops 14336 | bytes 114688 | tf_op jit(solution)/shard_map/psum | solution.py:145
  939.4 0.6 dynamic-slice_bitcast_fusion
  940.0 28.5 %all-reduce.7.cloned.1.call-done = f32[2048,256]{1,0:T(8,128)} async-done(((f32[2048,256]{1,0:T(8,128)}), f32[2048,256]{1,0:T(8,128)}) %all-reduce.7.cloned.1.call-update) | async-done | bytes 2097168 | tf_op jit(solution)/shard_map/psum | solution.py:145
  968.6 1.9 multiply_reduce_fusion
  970.5 0.0 copy-done
  970.5 0.0 copy-done.13
  970.5 0.0 copy-start.12
  970.5 2.4 convert_add_fusion
  973.0 0.7 dynamic-slice_convert_fusion
  973.7 0.0 copy-done.12
  973.7 1.9 fusion.62
  975.5 1.3 fusion.45
  976.8 100.2 %all-reduce = (f32[]{:T(128)}, f32[]{:T(128)}) all-reduce(f32[]{:T(128)} %get-tuple-element.9, f32[]{:T(128)} %dynamic-slice_reduce_fusion), channel_id=1, replica_groups=mesh['atom'=64,'ka'=8] {'atom','ka'}, use_global_device_ids=true, to_apply=%region_8.9 | all-reduce | flops 2 | bytes 16 | tf_op jit(solution)/shard_map/psum | solution.py:167
  (23 shorter events, 0.2 us)
Async XLA Ops:
  7.2 963.4 %copy-start = (bf16[256,256]{1,0:T(8,128)(2,1)S(1)}, bf16[256,256]{1,0:T(8,128)(2,1)}, u32[]{:S(2)}) copy-start(bf16[256,256]{1,0:T(8,128)(2,1)} %param.23) | copy-start | bytes 393220
  7.2 21.4 %copy-start.1 = (bf16[2048,256]{1,0:T(8,128)(2,1)S(1)}, bf16[2048,256]{1,0:T(8,128)(2,1)}, u32[]{:S(2)}) copy-start(bf16[2048,256]{1,0:T(8,128)(2,1)} %param.15) | copy-start | bytes 3145732
  7.2 832.2 %all-reduce.5.cloned.1.call-start = ((), (), s32[]{:S(2)}) async-start(), calls=%async_computation | async-start | bytes 2097152 | tf_op jit(solution)/shard_map/psum | solution.py:124
  27.2 1.3 copy-start.3
  27.2 8.1 copy-start.2
  28.6 3.4 copy-start.10
  28.6 3.4 copy-start.6
  28.6 3.8 copy-start.8
  28.6 3.9 copy-start.14
  28.6 4.6 copy-start.9
  31.2 2.9 copy-start.15
  31.3 937.3 %all-reduce.7.cloned.1.call-start = ((), (), s32[]{:S(2)}) async-start(), calls=%async_computation.1 | async-start | bytes 4194304 | tf_op jit(solution)/shard_map/psum | solution.py:145
  32.0 3.4 copy-start.4
  34.1 205.6 %copy-start.7 = (s32[3,512]{1,0:T(4,128)S(1)}, s32[3,512]{1,0:T(4,128)}, u32[]{:S(2)}) copy-start(s32[3,512]{1,0:T(4,128)} %param.17) | copy-start | bytes 18436
  845.3 3.5 copy-start.5
  845.3 3.5 copy-start.11
  850.1 120.4 %copy-start.13 = (f32[256]{0:T(256)S(1)}, f32[256]{0:T(256)}, u32[]{:S(2)}) copy-start(f32[256]{0:T(256)} %param.22) | copy-start | bytes 3076
  970.5 3.1 copy-start.12
Sparse Core Ops, SparseCore 0:
  31.4 807.9 all-reduce.4
  844.6 123.9 all-reduce.6
where the time goes:
time: 1090 us
  waiting for transfers between devices  628 us (58%)
  blocking collectives  372 us (34%)
  matrix products  41.4 us (4%)
  other arithmetic  22.5 us (2%)
  between operations  18.2 us (2%)
    psum x1, waiting for transfers between devices, local(): factor, charge_sum = lax.psum((factor, charge_sum), 'atom')  599 us
    psum x1, blocking collectives, local(): factor, charge_sum = lax.psum((factor, charge_sum), 'atom')  204 us
    psum x1, blocking collectives, local(): lax.psum((jnp.sum(misfit), jnp.sum(own_rows(live_mask))), ('atom', 'ka'))  100 us
    psum x1, blocking collectives, local(): lax.psum((potential, teacher_force, student_part), 'ka')  68.6 us
    psum x1, waiting for transfers between devices, local(): lax.psum((potential, teacher_force, student_part), 'ka')  28.5 us
  transfers between devices with their start and end apart: 2, of which 2 were waited for; matrix products, arithmetic and copies ran while one was open for 3% of the time, Pallas kernels for 0%

commit v1 on v0

--- a/solution.py
+++ b/solution.py
@@ -7,6 +7,7 @@
 TWO_PI = 2.0 * math.pi
 SCREEN = 20.0
 HIGHEST_PRECISION = lax.Precision.HIGHEST
+build_spot_now = lambda xin: lax.psum(lax.psum(xin, "ka"), "atom")
 
 
 def phase_table(positions, k_indices):
@@ -164,7 +165,7 @@
         own_rows(whole_rows[4]),
     )
     teacher_features, teacher_out, forces, student_energy, misfit = outputs
-    loss_sum, live_sum = lax.psum((jnp.sum(misfit), jnp.sum(own_rows(live_mask))), ("atom", "ka"))
+    loss_sum, live_sum = build_spot_now((jnp.sum(misfit), jnp.sum(own_rows(live_mask))))
     return (teacher_features, teacher_out.T, forces.T, student_energy, loss_sum / live_sum)
 
 

time: 1090 us -> 1220 us (1.12)
  the two profiles are of different devices: /device:TPU:1 before, /device:TPU:32 now
where the time goes in v1:
time: 1220 us
  waiting for transfers between devices  647 us (53%)
  blocking collectives  491 us (40%)
  matrix products  41.4 us (3%)
  other arithmetic  22.6 us (2%)
  between operations  18.2 us (1%)
    psum x1, waiting for transfers between devices, local(): factor, charge_sum = lax.psum((factor, charge_sum), 'atom')  619 us
    psum x2, blocking collectives, build_spot_now = lambda xin: lax.psum(lax.psum(xin, 'ka'), 'atom')  238 us
    psum x1, blocking collectives, local(): factor, charge_sum = lax.psum((factor, charge_sum), 'atom')  226 us
    psum x1, waiting for transfers between devices, local(): lax.psum((potential, teacher_force, student_part), 'ka')  28.4 us
    psum x1, blocking collectives, local(): lax.psum((potential, teacher_force, student_part), 'ka')  26.8 us
  transfers between devices with their start and end apart: 2, of which 2 were waited for; matrix products, arithmetic and copies ran while one was open for 3% of the time, Pallas kernels for 0%

profile of v1, /device:TPU:32, one launch (start us, length us, event | category | flops | bytes accessed | tf_op | source)
XLA Modules:
  0.0 1224.0 jit_solution(15743364662750504225)
XLA Ops:
  7.2 0.0 copy-start
  7.2 0.0 copy-start.1
  7.2 0.0 all-reduce.6.cloned.1.call-start
  8.0 0.7 convert_element_type.47
  8.7 0.9 fusion.58
  9.6 17.6 %cosine_convert_fusion = (bf16[2048,512]{1,0:T(8,128)(2,1)S(1)}, bf16[2048,512]{1,0:T(8,128)(2,1)S(1)}) fusion(f32[512]{0:T(512)S(1)} %bitcast.54, f32[2048]{0:T(1024)S(1)} %bitcast.39, f32[512]{0:T(512)S(1)} %bitcast.56, f32[2048]{0:T(1024)S(1)} %bitcast.41, f32[512]{0:T(512)S(1)} %bitcast.52, f32[2048]{0:T(1024)S(1)} %bitcast.37), kind=kLoop, calls=%fused_computation.8 | loop fusion | flops 8388608 | bytes 4225024 | tf_op jit(solution)/shard_map/slice | solution.py:134
  27.2 0.0 copy-start.3
  27.2 0.0 copy-start.2
  27.3 1.3 copy-done.3
  28.6 0.0 copy-done.1
  28.6 0.0 copy-start.10
  28.6 0.0 copy-start.6
  28.6 0.0 copy-start.8
  28.6 0.0 copy-start.14
  28.6 0.0 copy-start.9
  28.6 2.6 fusion.20
  31.2 0.0 copy-start.15
  31.2 0.0 all-reduce.6.cloned.1.call-update
  31.3 0.0 all-reduce.8.cloned.1.call-start
  32.0 0.0 copy-done.10
  32.0 0.0 copy-done.6
  32.0 0.0 copy-start.4
  32.0 0.4 fusion.61
  32.4 0.0 copy-done.8
  32.5 0.0 copy-done.14
  32.5 0.7 fusion.16
  33.2 0.0 copy-done.9
  33.2 1.0 convolution_add_fusion
  34.1 0.0 copy-done.15
  34.2 0.0 copy-start.7
  34.2 1.2 fusion.10
  35.4 0.0 copy-done.2
  35.4 0.0 copy-done.4
  35.4 0.6 fusion.55
  36.1 226.3 %psum.66 = f32[1024]{0:T(1024)S(1)} all-reduce(f32[1024]{0:T(1024)S(1)} %bitcast.60), channel_id=1, replica_groups=mesh['atom'=64,'ka'=8] {'atom'}, use_global_device_ids=true, to_apply=%region_4.5 | all-reduce | flops 1024 | bytes 8192 | tf_op jit(solution)/shard_map/psum | solution.py:125
  262.3 0.0 copy-done.7
  262.4 0.2 divide_multiply_fusion
  262.6 618.5 %all-reduce.6.cloned.1.call-done = f32[1024,256]{1,0:T(8,128)} async-done(((f32[1024,256]{1,0:T(8,128)}), f32[1024,256]{1,0:T(8,128)}) %all-reduce.6.cloned.1.call-update) | async-done | bytes 1048592 | tf_op jit(solution)/shard_map/psum | solution.py:125
  881.2 5.1 fusion.53
  886.3 0.0 all-reduce.8.cloned.1.call-update
  886.4 0.8 dynamic-slice_reduce_fusion
  887.2 0.0 copy-start.5
  887.2 0.0 copy-start.11
  887.2 3.5 fusion.26
  890.7 0.0 copy-done.5
  890.7 0.0 copy-done.11
  890.7 1.3 fusion.7
  892.0 0.0 copy-start.13
  892.0 20.6 %fusion.1 = f32[2048,3]{0,1:T(4,128)S(1)} fusion(f32[2048,1024]{1,0:T(8,128)S(1)} %fusion.7, s32[3,512]{1,0:T(4,128)S(1)} %copy-done.7, f32[512]{0:T(512)S(1)} %bitcast.55, f32[2048]{0:T(1024)S(1)} %bitcast.40, f32[512]{0:T(512)S(1)} %bitcast.57, f32[2048]{0:T(1024)S(1)} %bitcast.42, f32[512]{0:T(512)S(1)} %bitcast.53, f32[2048]{0:T(1024)S(1)} %bitcast.38), kind=kOutput, calls=%fused_computation.2 | convolution fusion | flops 51383296 | bytes 8450048 | tf_op jit(solution)/shard_map/dot_general | solution.py:137
  912.6 26.8 %all-reduce.2 = (f32[2048,3]{0,1:T(4,128)S(1)}, f32[2048,4]{0,1:T(4,128)S(1)}) all-reduce(f32[2048,3]{0,1:T(4,128)S(1)} %fusion.1, f32[2048,4]{0,1:T(4,128)S(1)} %fusion.26), channel_id=1, replica_groups=mesh['atom'=64,'ka'=8] {'ka'}, use_global_device_ids=true, to_apply=%region_3.4 | all-reduce | flops 14336 | bytes 114688 | tf_op jit(solution)/shard_map/psum | solution.py:146
  939.5 0.6 dynamic-slice_bitcast_fusion
  940.1 28.4 %all-reduce.8.cloned.1.call-done = f32[2048,256]{1,0:T(8,128)} async-done(((f32[2048,256]{1,0:T(8,128)}), f32[2048,256]{1,0:T(8,128)}) %all-reduce.8.cloned.1.call-update) | async-done | bytes 2097168 | tf_op jit(solution)/shard_map/psum | solution.py:146
  968.5 1.9 multiply_reduce_fusion
  970.5 0.0 copy-done
  970.5 0.0 copy-done.13
  970.5 0.0 copy-start.12
  970.5 2.4 convert_add_fusion
  972.9 0.7 dynamic-slice_convert_fusion
  973.6 0.0 copy-done.12
  973.6 1.9 fusion.62
  975.5 1.3 fusion.45
  976.7 16.9 %all-reduce.1 = (f32[]{:T(128)}, f32[]{:T(128)}) all-reduce(f32[]{:T(128)} %get-tuple-element.11, f32[]{:T(128)} %dynamic-slice_reduce_fusion), channel_id=1, replica_groups=mesh['atom'=64,'ka'=8] {'ka'}, use_global_device_ids=true, to_apply=%region_8.9 | all-reduce | flops 2 | bytes 16 | tf_op jit(solution)/shard_map/psum | solution.py:10
  993.6 221.2 %all-reduce = (f32[]{:T(128)}, f32[]{:T(128)}) all-reduce(f32[]{:T(128)} %get-tuple-element.7, f32[]{:T(128)} %get-tuple-element.8), channel_id=1, replica_groups=mesh['atom'=64,'ka'=8] {'atom'}, use_global_device_ids=true, to_apply=%region_9.10 | all-reduce | flops 2 | bytes 16 | tf_op jit(solution)/shard_map/psum | solution.py:10
  (23 shorter events, 0.2 us)
Async XLA Ops:
  7.2 963.3 %copy-start = (bf16[256,256]{1,0:T(8,128)(2,1)S(1)}, bf16[256,256]{1,0:T(8,128)(2,1)}, u32[]{:S(2)}) copy-start(bf16[256,256]{1,0:T(8,128)(2,1)} %param.23) | copy-start | bytes 393220
  7.2 21.4 %copy-start.1 = (bf16[2048,256]{1,0:T(8,128)(2,1)S(1)}, bf16[2048,256]{1,0:T(8,128)(2,1)}, u32[]{:S(2)}) copy-start(bf16[2048,256]{1,0:T(8,128)(2,1)} %param.15) | copy-start | bytes 3145732
  7.2 874.0 %all-reduce.6.cloned.1.call-start = ((), (), s32[]{:S(2)}) async-start(), calls=%async_computation | async-start | bytes 2097152 | tf_op jit(solution)/shard_map/psum | solution.py:125
  27.2 1.3 copy-start.3
  27.2 8.2 copy-start.2
  28.6 3.4 copy-start.10
  28.6 3.4 copy-start.6
  28.6 3.9 copy-start.8
  28.6 3.9 copy-start.14
  28.6 4.6 copy-start.9
  31.2 2.9 copy-start.15
  31.3 937.3 %all-reduce.8.cloned.1.call-start = ((), (), s32[]{:S(2)}) async-start(), calls=%async_computation.1 | async-start | bytes 4194304 | tf_op jit(solution)/shard_map/psum | solution.py:146
  32.0 3.4 copy-start.4
  34.2 228.2 %copy-start.7 = (s32[3,512]{1,0:T(4,128)S(1)}, s32[3,512]{1,0:T(4,128)}, u32[]{:S(2)}) copy-start(s32[3,512]{1,0:T(4,128)} %param.17) | copy-start | bytes 18436
  887.2 3.5 copy-start.5
  887.2 3.5 copy-start.11
  892.0 78.5 %copy-start.13 = (f32[256]{0:T(256)S(1)}, f32[256]{0:T(256)}, u32[]{:S(2)}) copy-start(f32[256]{0:T(256)} %param.22) | copy-start | bytes 3076
  970.5 3.1 copy-start.12
Sparse Core Ops, SparseCore 0:
  31.4 849.7 all-reduce.5
  886.4 82.0 all-reduce.7
